TPU v7x, 32 devices: a whole 2x2x4 slice. The times are simulated.
32 devices in a mesh: visit: 4 (over z), row: 2 (over core), col: 4 (over y, x).
Axes of the slice: x: 2, y: 2, z: 4, core: 2. Of those that a mesh axis runs over, the one named last changes fastest.
Arguments:
- images: bfloat16 [16, 1024, 2048], P('visit', 'row', 'col'), may hold values from -10 to 10, as said below
- coeffs: float32 [16, 3], P('visit'), may hold values from 0.3 to 1.2
- pair_list: int32 [8, 3], replicated, may hold values from 0 to 480, as said below
- weights: bfloat16 [16, 2, 4], P('visit', 'row', 'col'), may hold values from 0.5 to 4
- resample_bank: bfloat16 [12, 512, 512], replicated, may hold values from -0.25 to 0.25
- warp_index: int32 [16, 2, 4, 2], P('visit', 'row', 'col'), may hold values from 0 to 11
- destinations: int32 [16, 2, 4, 4], P('visit', 'row', 'col'), may hold values from 0 to 3, as said below
- counts: int32 [16, 2, 4], P('visit', 'row', 'col'), may hold values from 3 to 4
Outputs:
- coadd_patch: float32 [4, 1024, 2048], P('visit', 'row', 'col')
- plane_fit: float32 [16, 3], P('visit')
Inputs may be any that keep to these rules, and one draw needn't show every extreme that they name: `images`: noise plus a per-exposure sky plane. `pair_list`: every exposure appears in exactly one pair; offsets lie in 0 to 480, both ends used. `destinations`: the used entries of one tile's list are distinct; each tile lists the patch of its own visit index; a patch drawn with skew, which may be the device's own visit patch, is listed by all 4 tiles at each device position.
All inputs are finite; a program needn't handle non-finite values.
Results may differ from a plain program's by a relative error of at most 0.015.
Values may be sent and summed in bfloat16 or wider, within the bound.
No kernel may reach another device: no remote copies, remote signals or barrier semaphores. Data moves between devices by JAX's collectives and lax.ppermute only.
A program may use at most 192 MiB of HBM per device.

v0:
```python
import jax
import jax.numpy as jnp
from jax import lax
from jax.sharding import PartitionSpec as P

HALO = 16
STRIP = 32
MAXD = 4
SIGMA_PARTS = (0.0625, 0.125, 0.25)


def extended(value, sides, width):
    for axis, dim in sides:
        devices, length = (lax.axis_size(axis), value.shape[dim])
        up = [(i, (i + 1) % devices) for i in range(devices - 1)]
        down = [(j, i) for i, j in up]
        last = lax.slice_in_dim(value, length - width, length, axis=dim)
        initial = lax.slice_in_dim(value, 0, width, axis=dim)
        before = lax.ppermute(last, axis, up)
        after = lax.ppermute(initial, axis, down)
        value = jnp.concatenate([before, value, after], axis=dim)
    return value


def band_table(length, width, sigma):
    spread = (jnp.arange(2 * width + 1) - width).astype(jnp.float32)
    curve = jnp.exp(-spread * spread / (2.0 * sigma * sigma))
    total = jnp.sum(curve)
    rows_grid = lax.broadcasted_iota(jnp.int32, (length, length + 2 * width), 0)
    cols_grid = lax.broadcasted_iota(jnp.int32, (length, length + 2 * width), 1)
    offset = (cols_grid - rows_grid - width).astype(jnp.float32)
    values = jnp.exp(-offset * offset / (2.0 * sigma * sigma)) / total
    return jnp.where(jnp.abs(offset) <= width, values, 0.0).astype(jnp.bfloat16)


def centred(index, length):
    return (index.astype(jnp.float32) + 0.5) / length * 2.0 - 1.0


def solve_three(normal, moments):
    lower = jnp.linalg.cholesky(normal)
    first = moments[..., 0] / lower[..., 0, 0]
    second = (moments[..., 1] - lower[..., 1, 0] * first) / lower[..., 1, 1]
    third = (moments[..., 2] - lower[..., 2, 0] * first - lower[..., 2, 1] * second) / lower[
        ..., 2, 2
    ]
    upper_top = third / lower[..., 2, 2]
    upper_mid = (second - lower[..., 2, 1] * upper_top) / lower[..., 1, 1]
    upper_low = (first - lower[..., 1, 0] * upper_mid - lower[..., 2, 0] * upper_top) / lower[
        ..., 0, 0
    ]
    return jnp.stack([upper_low, upper_mid, upper_top], -1)


def rows_from(source, anchor):
    return lax.dynamic_slice_in_dim(source, anchor, STRIP, 0)


def shards(images, coeffs, pair_list, weights, resample_bank, warp_index, destinations, counts):
    exp_dev = images.shape[0]
    tile_len = images.shape[1]
    row_count = lax.axis_size("row")
    col_count = lax.axis_size("col")
    visit_count = lax.axis_size("visit")
    row_pos = lax.axis_index("row")
    col_pos = lax.axis_index("col")
    visit_pos = lax.axis_index("visit")
    height = row_count * tile_len
    breadth = col_count * tile_len
    padded = extended(images, (("row", 1), ("col", 2)), HALO)
    matched = jnp.zeros((exp_dev, tile_len, tile_len), jnp.float32)
    for kernel in range(len(SIGMA_PARTS)):
        table = band_table(tile_len, HALO, HALO * SIGMA_PARTS[kernel])
        across = jnp.einsum(
            "ij,ejl->eil", table, padded, preferred_element_type=jnp.float32
        ).astype(jnp.bfloat16)
        smoothed = jnp.einsum("eil,ml->eim", across, table, preferred_element_type=jnp.float32)
        matched = matched + coeffs[:, kernel, None, None] * smoothed
    own_ids = visit_pos * exp_dev + jnp.arange(exp_dev, dtype=jnp.int32)
    first_col = pair_list[:, 0]
    second_col = pair_list[:, 1]
    offsets = pair_list[:, 2]
    hit_first = first_col[None, :] == own_ids[:, None]
    hit_second = second_col[None, :] == own_ids[:, None]
    partner = jnp.sum(
        jnp.where(hit_first, second_col[None, :], 0) + jnp.where(hit_second, first_col[None, :], 0),
        axis=1,
    )
    offset = jnp.sum(jnp.where(hit_first | hit_second, offsets[None, :], 0), axis=1)
    own_strip = jax.vmap(rows_from)(images, offset)
    everyone = lax.all_gather(own_strip, "visit", axis=0, tiled=True)
    theirs = jnp.take(everyone, partner, axis=0).astype(jnp.float32)
    nearby = jax.vmap(rows_from)(matched, offset)
    difference = nearby - theirs
    pixel_weight = 1.0 / (1.0 + theirs * theirs)
    strip_rows = row_pos * tile_len + offset[:, None] + jnp.arange(STRIP, dtype=jnp.int32)[None, :]
    ycoord = centred(strip_rows, height)[:, :, None]
    xcoord = centred(col_pos * tile_len + jnp.arange(tile_len, dtype=jnp.int32), breadth)
    xgrid = xcoord[None, None, :]
    weight_x = pixel_weight * xgrid
    weight_y = pixel_weight * ycoord
    sum_w = jnp.sum(pixel_weight, axis=(1, 2))
    sum_x = jnp.sum(weight_x, axis=(1, 2))
    sum_y = jnp.sum(weight_y, axis=(1, 2))
    sum_xx = jnp.sum(weight_x * xgrid, axis=(1, 2))
    sum_xy = jnp.sum(weight_x * ycoord, axis=(1, 2))
    sum_yy = jnp.sum(weight_y * ycoord, axis=(1, 2))
    normal = jnp.stack(
        [
            jnp.stack([sum_w, sum_x, sum_y], -1),
            jnp.stack([sum_x, sum_xx, sum_xy], -1),
            jnp.stack([sum_y, sum_xy, sum_yy], -1),
        ],
        1,
    )
    moments = jnp.stack(
        [
            jnp.sum(pixel_weight * difference, axis=(1, 2)),
            jnp.sum(weight_x * difference, axis=(1, 2)),
            jnp.sum(weight_y * difference, axis=(1, 2)),
        ],
        -1,
    )
    normal, moments = lax.psum((normal, moments), ("row", "col"))
    plane_fit = solve_three(normal, moments)
    row_coord = centred(row_pos * tile_len + jnp.arange(tile_len, dtype=jnp.int32), height)
    background = (
        plane_fit[:, 0, None, None]
        + plane_fit[:, 1, None, None] * xcoord[None, None, :]
        + plane_fit[:, 2, None, None] * row_coord[None, :, None]
    )
    corrected = (matched - background).astype(jnp.bfloat16)
    choose = warp_index[:, 0, 0, :]
    row_maps = jnp.take(resample_bank, choose[:, 0], axis=0)
    col_maps = jnp.take(resample_bank, choose[:, 1], axis=0)
    halfway = jnp.einsum(
        "eij,ejk->eik", row_maps, corrected, preferred_element_type=jnp.float32
    ).astype(jnp.bfloat16)
    warped = jnp.einsum(
        "eik,elk->eil", halfway, col_maps, preferred_element_type=jnp.float32
    ).astype(jnp.bfloat16)
    listed = destinations[:, 0, 0, :]
    how_many = counts[:, 0, 0]
    usable = jnp.arange(MAXD, dtype=jnp.int32)[None, :] < how_many[:, None]
    owners = jnp.arange(visit_count, dtype=jnp.int32)
    member = jnp.any(usable[:, :, None] & (listed[:, :, None] == owners[None, None, :]), axis=1)
    tile_weight = weights[:, 0, 0]
    nothing = jnp.zeros((), jnp.bfloat16)
    picked = jnp.where(member, tile_weight[:, None], nothing)
    partial_sum = jnp.einsum("ev,eij->vij", picked, warped, preferred_element_type=jnp.float32)
    partial_weight = jnp.sum(picked.astype(jnp.float32), axis=0)
    numerator, denominator = (
        lax.psum_scatter(
            partial_sum.astype(jnp.bfloat16), "visit", scatter_dimension=0, tiled=True
        ).astype(jnp.float32),
        lax.psum_scatter(
            partial_weight.astype(jnp.bfloat16), "visit", scatter_dimension=0, tiled=True
        ).astype(jnp.float32),
    )
    coadd_patch = numerator / denominator[:, None, None]
    return (coadd_patch, plane_fit)


def solution(mesh):
    in_specs = (
        P("visit", "row", "col"),
        P("visit", None),
        P(),
        P("visit", "row", "col"),
        P(),
        P("visit", "row", "col", None),
        P("visit", "row", "col", None),
        P("visit", "row", "col"),
    )
    out_specs = (P("visit", "row", "col"), P("visit", None))
    return jax.shard_map(shards, mesh=mesh, in_specs=in_specs, out_specs=out_specs, check_vma=False)
```

profile of v0, /device:TPU:0, one launch (start us, length us, event | category | flops | bytes accessed | tf_op | source)
XLA Modules:
  0.0 194.2 jit_solution(17051824752516389986)
XLA Ops:
  7.2 0.0 reduce-scatter.2.cloned.1.call-start
  7.2 0.9 fusion.128
  8.1 1.0 copy.60
  9.1 2.4 %collective-permute-start = (bf16[4,16,512]{1,2,0:T(8,128)(2,1)}, bf16[4,16,512]{1,2,0:T(8,128)(2,1)S(1)}, u32[]{:S(2)}, u32[]{:S(2)}) collective-permute-start(bf16[4,16,512]{1,2,0:T(8,128)(2,1)} %copy.60), channel_id=1, source_target_pairs={{0,4},{1,5},{2,6},{3,7},{8,12},{9,13},{10,14},{11,15},{16,20},{17,... | collective-permute-start | bytes 196616 | tf_op jit(solution)/shard_map/ppermute | solution.py:19
  11.5 1.0 copy.61
  12.5 1.4 collective-permute-start.1
  13.9 4.2 %copy.62 = bf16[4,512,512]{1,2,0:T(8,128)(2,1)} copy(bf16[4,512,512]{2,1,0:T(8,128)(2,1)} %param.10) | data formatting | bytes 4194304 | tf_op args[0]
  18.1 0.6 exponential_reduce_fusion.1
  18.7 0.6 exponential_reduce_fusion
  19.3 0.6 exponential_reduce_fusion.2
  19.9 0.0 copy-done
  19.9 2.9 %copy.63 = bf16[4,512,512]{2,0,1:T(4,128)(2,1)} copy(bf16[4,512,512]{2,1,0:T(8,128)(2,1)S(1)} %copy-done) | data formatting | bytes 4194304 | tf_op args[0]
  22.8 0.0 copy-done.5
  22.9 0.2 fusion.81
  23.1 0.2 slice_reduce_fusion.2
  23.3 1.9 gather_fusion.1
  25.2 17.4 %all_gather.3 = bf16[16,32,512]{2,1,0:T(8,128)(2,1)S(1)} all-gather(bf16[4,32,512]{2,1,0:T(8,128)(2,1)S(1)} %copy.64), channel_id=1, replica_groups=mesh['visit'=4,'row'=2,'col'=4] {'visit'}, dimensions={0}, use_global_device_ids=true | all-gather | bytes 655360 | tf_op jit(solution)/shard_map/all_gather | solution.py:91
  42.6 0.1 multiply_add_fusion.3
  42.7 4.8 %gather_fusion.3 = bf16[4,512,512]{2,1,0:T(8,128)(2,1)} fusion(bf16[12,512,512]{2,1,0:T(8,128)(2,1)} %param.14, s32[1024]{0:T(1024)S(1)} %get-tuple-element.65), kind=kCustom, calls=%fused_computation.clone | custom fusion | bytes 4194320 | tf_op jit(solution)/shard_map/jit(_take)/gather | solution.py:134
  47.5 5.0 %gather_fusion.4 = bf16[4,512,512]{2,1,0:T(8,128)(2,1)} fusion(bf16[12,512,512]{2,1,0:T(8,128)(2,1)} %param.14, s32[1024]{0:T(1024)S(1)} %get-tuple-element.64), kind=kCustom, calls=%fused_computation.1.clone | custom fusion | bytes 4194320 | tf_op jit(solution)/shard_map/jit(_take)/gather | solution.py:135
  52.5 0.1 iota_compare_fusion.3
  52.5 0.6 gather_fusion
  53.1 0.0 copy-done.4
  53.1 0.1 fusion.79
  53.2 0.0 collective-permute-done
  53.2 0.0 collective-permute-done.1
  53.3 0.9 pad_maximum_fusion.3
  54.1 3.4 %collective-permute-start.2 = (bf16[4,544,16]{1,2,0:T(8,128)(2,1)S(1)}, bf16[4,544,16]{1,2,0:T(8,128)(2,1)S(1)}, u32[]{:S(2)}, u32[]{:S(2)}) collective-permute-start(bf16[4,544,16]{1,2,0:T(8,128)(2,1)S(1)} %get-tuple-element.49), channel_id=1, source_target_pairs={{0,1},{1,2},{2,3},{4,5},{5,6},{6,7},{8,9},{9,10},{10,11},{12,13},{... | collective-permute-start | bytes 208904 | tf_op jit(solution)/shard_map/ppermute | solution.py:19
  57.5 1.5 collective-permute-start.3
  59.0 0.6 collective-permute-done.2
  59.6 4.2 %collective-permute-done.3 = bf16[4,544,16]{1,2,0:T(8,128)(2,1)S(1)} collective-permute-done((bf16[4,544,16]{1,2,0:T(8,128)(2,1)S(1)}, bf16[4,544,16]{1,2,0:T(8,128)(2,1)S(1)}, u32[]{:S(2)}, u32[]{:S(2)}) %collective-permute-start.3) | collective-permute-done | bytes 69664 | tf_op jit(solution)/shard_map/ppermute | solution.py:20
  63.9 7.6 %fusion.2 = f32[4,512,512]{2,1,0:T(8,128)} fusion(f32[]{:T(128)} %exponential_reduce_fusion.1, bf16[4,544,16]{1,2,0:T(8,128)(2,1)S(1)} %collective-permute-done.3, bf16[4,16,512]{1,2,0:T(8,128)(2,1)} %collective-permute-done.1, bf16[4,512,512]{1,2,0:T(8,128)(2,1)S(1)} %copy-done.1, bf16[4,16,512]{1,2,0:T(8,128)(2,1)S(1)} %collective-permute-done, ...), kind=kOutput, calls=%fused_computation.10 | convolution fusion | flops 2372083712 | bytes 6561796 | tf_op jit(solution)/shard_map/eil,ml->eim/dot_general | solution.py:77
  71.4 7.7 %fusion = f32[4,512,512]{2,1,0:T(8,128)} fusion(f32[]{:T(128)} %exponential_reduce_fusion, bf16[4,544,16]{1,2,0:T(8,128)(2,1)S(1)} %collective-permute-done.3, bf16[4,16,512]{1,2,0:T(8,128)(2,1)} %collective-permute-done.1, bf16[4,512,512]{1,2,0:T(8,128)(2,1)S(1)} %copy-done.1, bf16[4,16,512]{1,2,0:T(8,128)(2,1)S(1)} %collective-permute-done, ...), kind=kOutput, calls=%fused_computation.8 | convolution fusion | flops 2372083712 | bytes 6561796 | tf_op jit(solution)/shard_map/eil,ml->eim/dot_general | solution.py:77
  79.1 9.8 %multiply_add_fusion = f32[4,512,512]{2,1,0:T(8,128)} fusion(f32[4,512,512]{2,1,0:T(8,128)} %fusion, f32[4,512,512]{2,1,0:T(8,128)} %fusion.2, f32[4]{0:T(128)S(1)} %get-tuple-element.30, f32[4]{0:T(128)S(1)} %get-tuple-element.31, f32[4]{0:T(128)S(1)} %get-tuple-element.29, f32[]{:T(128)} %exponential_reduce_fusion.2, ...), kind=kOutput, calls=%fused_computation.6 | convolution fusion | flops 2377326592 | bytes 14950452 | tf_op jit(solution)/shard_map/eil,ml->eim/dot_general | solution.py:77
  88.9 6.8 %copy.65 = f32[4,512,512]{2,0,1:T(4,128)} copy(f32[4,512,512]{2,1,0:T(8,128)} %multiply_add_fusion) | data formatting | bytes 8388608 | tf_op jit(solution)/shard_map/add | solution.py:78
  95.7 1.9 gather_fusion.2
  97.7 0.4 multiply_reduce_fusion.5
  98.1 0.1 copy.70
  98.2 0.1 copy.71
  98.3 0.1 copy.72
  98.5 0.1 pad_maximum_fusion.4
  98.5 27.4 %all-reduce.2 = (f32[4,3,3]{1,2,0:T(4,128)S(1)}, f32[4,3]{0,1:T(4,128)S(1)}) all-reduce(f32[4,3,3]{1,2,0:T(4,128)S(1)} %pad_maximum_fusion.4, f32[4,3]{0,1:T(4,128)S(1)} %pad_maximum_fusion.5), channel_id=1, replica_groups=mesh['visit'=4,'row'=2,'col'=4] {'row','col'}, use_global_device_ids=true, to_apply=%region_16.18 | all-reduce | flops 48 | bytes 384 | tf_op jit(solution)/shard_map/psum | solution.py:124
  125.9 0.1 copy.73
  126.0 1.1 custom-call.4
  127.2 0.1 compare_reduce_fusion
  127.3 0.1 copy.74
  127.4 0.1 copy.75
  127.5 0.1 copy.76
  127.6 0.1 select_select_fusion
  127.7 0.1 subtract_divide_fusion.3
  127.8 0.1 subtract_divide_fusion.1
  127.9 0.2 slice_reduce_fusion.4
  128.1 0.1 multiply_add_fusion.1
  128.1 6.7 %fusion.22 = bf16[4,512,512]{2,1,0:T(8,128)(2,1)} fusion(bf16[4,512,512]{2,1,0:T(8,128)(2,1)} %gather_fusion.4, pred[4]{0:T(512)(128)(4,1)S(1)} %get-tuple-element.59, f32[4,512,512]{2,1,0:T(8,128)} %multiply_add_fusion, bf16[4,512,512]{2,1,0:T(8,128)(2,1)S(1)} %copy-done.2, f32[4,512]{1,0:T(4,128)S(1)} %get-tuple-element.67, ...), kind=kOutput, calls=%fused_computation.28 | convolution fusion | flops 2154823680 | bytes 10502152 | tf_op jit(solution)/shard_map/eik,elk->eil/dot_general | solution.py:139
  134.8 4.0 %fusion.27 = bf16[4,512,512]{2,0,1:T(4,128)(2,1)S(1)} fusion(bf16[4,512,512]{2,1,0:T(8,128)(2,1)} %fusion.22, pred[4,4]{1,0:T(4,128)(4,1)S(1)} %fusion.79, bf16[4]{0:T(256)(128)(2,1)S(1)} %bitcast.139), kind=kOutput, calls=%fused_computation.29 | convolution fusion | flops 9437200 | bytes 4194328 | tf_op jit(solution)/shard_map/ev,eij->vij/dot_general | solution.py:150
  138.8 1.8 copy.79
  140.6 0.0 reduce-scatter.2.cloned.1.call-update
  140.6 0.1 select_reduce_fusion.2
  140.7 11.5 %all-reduce.1 = bf16[4]{0:T(256)(128)(2,1)S(1)} all-reduce(bf16[4]{0:T(256)(128)(2,1)S(1)} %select_reduce_fusion.2), channel_id=3, replica_groups=mesh['visit'=4,'row'=2,'col'=4] {'visit'}, use_global_device_ids=true, to_apply=%region_21.23.clone | all-reduce | flops 4 | bytes 16
  152.2 0.6 dynamic-slice
  152.8 1.2 dynamic-slice.1
  154.7 0.7 copy.80
  155.4 29.8 %reduce-scatter.2.cloned.1.call-done = bf16[1,512,512]{2,1,0:T(8,128)(2,1)} async-done(((bf16[4,512,512]{2,1,0:T(8,128)(2,1)}), bf16[1,512,512]{2,1,0:T(8,128)(2,1)}) %reduce-scatter.2.cloned.1.call-update) | async-done | bytes 524304 | tf_op jit(solution)/shard_map/reduce_scatter | solution.py:153
  185.2 2.2 %convert_divide_fusion = f32[1,512,512]{2,1,0:T(8,128)} fusion(bf16[1,512,512]{2,1,0:T(8,128)(2,1)} %reduce-scatter.2.cloned.1.call-done, f32[]{:T(128)S(6)} %convert.2), kind=kLoop, calls=%fused_computation.40 | loop fusion | flops 524288 | bytes 1572868 | tf_op jit(solution)/shard_map/div | solution.py:160
  (39 shorter events, 0.3 us)
Async XLA Ops:
  7.2 178.1 %reduce-scatter.2.cloned.1.call-start = ((), (), s32[]{:S(2)}) async-start(), calls=%async_computation.1 | async-start | bytes 2621440 | tf_op jit(solution)/shard_map/reduce_scatter | solution.py:153
  9.1 44.1 %collective-permute-start = (bf16[4,16,512]{1,2,0:T(8,128)(2,1)}, bf16[4,16,512]{1,2,0:T(8,128)(2,1)S(1)}, u32[]{:S(2)}, u32[]{:S(2)}) collective-permute-start(bf16[4,16,512]{1,2,0:T(8,128)(2,1)} %copy.60), channel_id=1, source_target_pairs={{0,4},{1,5},{2,6},{3,7},{8,12},{9,13},{10,14},{11,15},{16,20},{17,... | collective-permute-start | bytes 196616 | tf_op jit(solution)/shard_map/ppermute | solution.py:19
  12.5 7.4 %copy-start = (bf16[4,512,512]{2,1,0:T(8,128)(2,1)S(1)}, bf16[4,512,512]{2,1,0:T(8,128)(2,1)}, u32[]{:S(2)}) copy-start(bf16[4,512,512]{2,1,0:T(8,128)(2,1)} %param.10) | copy-start | bytes 6291460
  12.5 40.7 %collective-permute-start.1 = (bf16[4,16,512]{1,2,0:T(8,128)(2,1)}, bf16[4,16,512]{1,2,0:T(8,128)(2,1)}, u32[]{:S(2)}, u32[]{:S(2)}) collective-permute-start(bf16[4,16,512]{1,2,0:T(8,128)(2,1)} %copy.61), channel_id=1, source_target_pairs={{4,0},{5,1},{6,2},{7,3},{12,8},{13,9},{14,10},{15,11},{20,16},{21,... | collective-permute-start | bytes 196616 | tf_op jit(solution)/shard_map/ppermute | solution.py:20
  19.9 2.9 %copy-start.5 = (s32[8,3]{0,1:T(4,128)S(1)}, s32[8,3]{0,1:T(4,128)}, u32[]{:S(2)}) copy-start(s32[8,3]{0,1:T(4,128)} %param.12) | copy-start | bytes 292
  19.9 3.2 %copy-start.3 = (f32[4,3]{1,0:T(4,128)S(1)}, f32[4,3]{1,0:T(4,128)}, u32[]{:S(2)}) copy-start(f32[4,3]{1,0:T(4,128)} %param.11) | copy-start | bytes 148
  22.8 19.8 %copy-start.6 = (s32[4,1,1,2]{0,3,2,1:T(2,128)S(1)}, s32[4,1,1,2]{0,3,2,1:T(2,128)}, u32[]{:S(2)}) copy-start(s32[4,1,1,2]{0,3,2,1:T(2,128)} %param.15) | copy-start | bytes 100
  47.5 5.0 %copy-start.7 = (s32[4,1,1]{0,2,1:T(1,128)S(1)}, s32[4,1,1]{0,2,1:T(1,128)}, u32[]{:S(2)}) copy-start(s32[4,1,1]{0,2,1:T(1,128)} %param.17) | copy-start | bytes 52
  47.5 5.6 %copy-start.4 = (s32[4,1,1,4]{3,2,1,0:T(1,128)S(1)}, s32[4,1,1,4]{3,2,1,0:T(1,128)}, u32[]{:S(2)}) copy-start(s32[4,1,1,4]{3,2,1,0:T(1,128)} %param.16) | copy-start | bytes 196
  47.5 5.8 %copy-start.1 = (bf16[4,512,512]{1,2,0:T(8,128)(2,1)S(1)}, bf16[4,512,512]{1,2,0:T(8,128)(2,1)}, u32[]{:S(2)}) copy-start(bf16[4,512,512]{1,2,0:T(8,128)(2,1)} %copy.62) | copy-start | bytes 6291460
  54.1 5.5 %collective-permute-start.2 = (bf16[4,544,16]{1,2,0:T(8,128)(2,1)S(1)}, bf16[4,544,16]{1,2,0:T(8,128)(2,1)S(1)}, u32[]{:S(2)}, u32[]{:S(2)}) collective-permute-start(bf16[4,544,16]{1,2,0:T(8,128)(2,1)S(1)} %get-tuple-element.49), channel_id=1, source_target_pairs={{0,1},{1,2},{2,3},{4,5},{5,6},{6,7},{8,9},{9,10},{10,11},{12,13},{... | collective-permute-start | bytes 208904 | tf_op jit(solution)/shard_map/ppermute | solution.py:19
  57.5 6.3 %collective-permute-start.3 = (bf16[4,544,16]{1,2,0:T(8,128)(2,1)S(1)}, bf16[4,544,16]{1,2,0:T(8,128)(2,1)S(1)}, u32[]{:S(2)}, u32[]{:S(2)}) collective-permute-start(bf16[4,544,16]{1,2,0:T(8,128)(2,1)S(1)} %get-tuple-element.50), channel_id=1, source_target_pairs={{1,0},{2,1},{3,2},{5,4},{6,5},{7,6},{9,8},{10,9},{11,10},{13,12},{... | collective-permute-start | bytes 208904 | tf_op jit(solution)/shard_map/ppermute | solution.py:20
  95.7 32.4 %copy-start.2 = (bf16[4,512,512]{2,1,0:T(8,128)(2,1)S(1)}, bf16[4,512,512]{2,1,0:T(8,128)(2,1)}, u32[]{:S(2)}) copy-start(bf16[4,512,512]{2,1,0:T(8,128)(2,1)} %gather_fusion.3) | copy-start | bytes 6291460
  128.1 6.7 %copy-start.8 = (bf16[4,1,1]{0,2,1:T(2,128)(2,1)S(1)}, bf16[4,1,1]{0,2,1:T(2,128)(2,1)}, u32[]{:S(2)}) copy-start(bf16[4,1,1]{0,2,1:T(2,128)(2,1)} %param.13) | copy-start | bytes 28
  140.6 11.6 %copy-start.9 = (u32[32]{0:T(128)S(1)}, u32[32]{0:T(128)}, u32[]{:S(2)}) copy-start(u32[32]{0:T(128)} %constant.184) | copy-start | bytes 388
Sparse Core Ops, SparseCore 0:
  140.7 44.4 reduce-scatter.1
where the time goes:
time: 195 us; the launch traced here: 194 us
  blocking collectives  56.3 us (29%)
  local copies, waits for them, and re-layouts  36.1 us (19%)
  matrix products  35.7 us (18%)
  waiting for transfers between devices  34.7 us (18%)
  between operations  14.9 us (8%)
  starting transfers between devices  8.7 us (4%)
  other arithmetic  7.86 us (4%)
    reduce_scatter x1, waiting for transfers between devices, shards(): lax.psum_scatter(partial_sum.astype(jnp.bfloat16), 'visit', scatter_dimen...  29.8 us
    psum x1, blocking collectives, shards(): normal, moments = lax.psum((normal, moments), ('row', 'col'))  27.4 us
    dot_general x3, matrix products, shards(): jnp.einsum('eil,ml->eim', across, table, preferred_element_type=jnp.float32)  25 us
    all_gather x1, blocking collectives, shards(): everyone = lax.all_gather(own_strip, 'visit', axis=0, tiled=True)  17.4 us
    unnamed x1, blocking collectives  11.5 us
    unnamed x25, local copies, waits for them, and re-layouts  9.58 us
    add x1, local copies, waits for them, and re-layouts, shards(): matched = matched + coeffs[:, kernel, None, None] * smoothed  6.81 us
    dot_general x1, matrix products, shards(): jnp.einsum('eik,elk->eil', halfway, col_maps, preferred_element_type=jnp....  6.68 us
  transfers between devices with their start and end apart: 5, of which 3 were waited for; matrix products, arithmetic and copies ran while one was open for 13% of the time, Pallas kernels for 0%

commit v1 on v0

--- a/solution.py
+++ b/solution.py
@@ -2,11 +2,18 @@
 import jax.numpy as jnp
 from jax import lax
 from jax.sharding import PartitionSpec as P
+from jax.lax import axis_index, axis_size, ppermute
 
 HALO = 16
 STRIP = 32
 MAXD = 4
 SIGMA_PARTS = (0.0625, 0.125, 0.25)
+
+
+def clear_pieces_all(row_data, k_dim):
+    v_next = list(row_data.shape[1:])
+    v_next[k_dim] *= row_data.shape[0]
+    return jnp.moveaxis(row_data, 0, k_dim).reshape(v_next)
 
 
 def extended(value, sides, width):
@@ -88,7 +95,22 @@
     )
     offset = jnp.sum(jnp.where(hit_first | hit_second, offsets[None, :], 0), axis=1)
     own_strip = jax.vmap(rows_from)(images, offset)
-    everyone = lax.all_gather(own_strip, "visit", axis=0, tiled=True)
+
+    def lead_vector(xs, axis_name, pos_dim):
+        num_devices = axis_size(axis_name)
+        panels = []
+        q = 0
+        while q < num_devices:
+            panels.append((q, (q + 1) % num_devices))
+            q += 1
+        store = [xs]
+        while len(store) < num_devices:
+            store.append(ppermute(store[-1], axis_name, panels))
+        formed = axis_index(axis_name)
+        store = jnp.stack(store)[(formed - jnp.arange(num_devices)) % num_devices]
+        return clear_pieces_all(store, pos_dim)
+
+    everyone = lead_vector(own_strip, "visit", 0)
     theirs = jnp.take(everyone, partner, axis=0).astype(jnp.float32)
     nearby = jax.vmap(rows_from)(matched, offset)
     difference = nearby - theirs

time: 195 us -> 188 us (0.964)
  blocking collectives: 56.3 us -> 38.1 us
  other arithmetic: 7.86 us -> 13.8 us
  starting transfers between devices: 8.7 us -> 14.2 us
  waiting for transfers between devices: 34.7 us -> 32.6 us
  local copies, waits for them, and re-layouts: 36.1 us -> 38.1 us
    all_gather x1 -> x0, blocking collectives: 17.4 us -> none  [shards(): everyone = lax.all_gather(own_strip, 'visit', axis=0, tiled=True)]
    ppermute x0 -> x3, starting transfers between devices: none -> 5.83 us  [lead_vector(): store.append(ppermute(store[-1], axis_name, panels))]
    unnamed x25 -> x37, local copies, waits for them, and re-layouts: 9.58 us -> 10.3 us
  transfers between devices with their start and end apart: 5 -> 8, of which waited for: 3 -> 2; matrix products, arithmetic and copies ran while one was open for 13% -> 33% of each run, Pallas kernels for 0% -> 0%
where the time goes in v1:
time: 188 us; the launch traced here: 187 us
  local copies, waits for them, and re-layouts  38.1 us (20%)
  blocking collectives  38.1 us (20%)
  matrix products  35.3 us (19%)
  waiting for transfers between devices  32.6 us (17%)
  between operations  14.9 us (8%)
  starting transfers between devices  14.2 us (8%)
  other arithmetic  13.8 us (7%)
    reduce_scatter x1, waiting for transfers between devices, shards(): lax.psum_scatter(partial_sum.astype(jnp.bfloat16), 'visit', scatter_dimen...  29.8 us
    psum x1, blocking collectives, shards(): normal, moments = lax.psum((normal, moments), ('row', 'col'))  27.4 us
    dot_general x3, matrix products, shards(): jnp.einsum('eil,ml->eim', across, table, preferred_element_type=jnp.float32)  24.6 us
    unnamed x1, blocking collectives  10.7 us
    unnamed x37, local copies, waits for them, and re-layouts  10.3 us
    add x1, local copies, waits for them, and re-layouts, shards(): matched = matched + coeffs[:, kernel, None, None] * smoothed  6.81 us
    dot_general x1, matrix products, shards(): jnp.einsum('eik,elk->eil', halfway, col_maps, preferred_element_type=jnp....  6.69 us
    ppermute x3, starting transfers between devices, lead_vector(): store.append(ppermute(store[-1], axis_name, panels))  5.83 us
  transfers between devices with their start and end apart: 8, of which 2 were waited for; matrix products, arithmetic and copies ran while one was open for 33% of the time, Pallas kernels for 0%

profile of v1, /device:TPU:0, one launch (start us, length us, event | category | flops | bytes accessed | tf_op | source)
XLA Modules:
  0.0 187.0 jit_solution(12398171341446810850)
XLA Ops:
  7.2 0.9 fusion.130
  8.1 1.0 copy.60
  9.1 2.4 %collective-permute-start = (bf16[4,16,512]{1,2,0:T(8,128)(2,1)}, bf16[4,16,512]{1,2,0:T(8,128)(2,1)S(1)}, u32[]{:S(2)}, u32[]{:S(2)}) collective-permute-start(bf16[4,16,512]{1,2,0:T(8,128)(2,1)} %copy.60), channel_id=1, source_target_pairs={{0,4},{1,5},{2,6},{3,7},{8,12},{9,13},{10,14},{11,15},{16,20},{17,... | collective-permute-start | bytes 196616 | tf_op jit(solution)/shard_map/ppermute | solution.py:26
  11.5 1.0 copy.61
  12.5 1.3 collective-permute-start.1
  13.8 4.7 %copy.63 = bf16[4,512,512]{2,0,1:T(4,128)(2,1)} copy(bf16[4,512,512]{2,1,0:T(8,128)(2,1)} %param.10) | data formatting | bytes 4194304 | tf_op args[0]
  18.5 0.2 fusion.81
  18.7 1.9 gather_fusion.2
  20.6 2.5 %collective-permute-start.4 = (bf16[4,32,512]{2,0,1:T(4,128)(2,1)S(1)}, bf16[4,32,512]{2,0,1:T(4,128)(2,1)S(1)}, u32[]{:S(2)}, u32[]{:S(2)}) collective-permute-start(bf16[4,32,512]{2,0,1:T(4,128)(2,1)S(1)} %gather_fusion.2), channel_id=1, source_target_pairs={{0,8},{8,16},{16,24},{24,0},{1,9},{9,17},{17,25},{25,1},{2,10},{10... | collective-permute-start | bytes 393224 | tf_op jit(solution)/shard_map/ppermute | solution.py:108
  23.1 2.4 %copy.62 = bf16[4,512,512]{1,2,0:T(8,128)(2,1)} copy(bf16[4,512,512]{2,1,0:T(8,128)(2,1)S(1)} %copy-done) | data formatting | bytes 4194304 | tf_op args[0]
  25.5 0.6 exponential_reduce_fusion.1
  26.1 0.6 exponential_reduce_fusion
  26.7 0.6 exponential_reduce_fusion.2
  27.4 0.5 compare_and_fusion.2
  28.0 0.2 slice_reduce_fusion.2
  28.1 0.6 pad_clamp_fusion.2
  28.7 0.6 pad_clamp_fusion.1
  29.4 0.5 compare_and_fusion.1
  30.0 4.8 %gather_fusion.4 = bf16[4,512,512]{2,1,0:T(8,128)(2,1)} fusion(bf16[12,512,512]{2,1,0:T(8,128)(2,1)} %param.14, s32[1024]{0:T(1024)S(1)} %get-tuple-element.65), kind=kCustom, calls=%fused_computation.clone | custom fusion | bytes 4194320 | tf_op jit(solution)/shard_map/jit(_take)/gather | solution.py:156
  34.7 5.0 %gather_fusion.5 = bf16[4,512,512]{2,1,0:T(8,128)(2,1)} fusion(bf16[12,512,512]{2,1,0:T(8,128)(2,1)} %param.14, s32[1024]{0:T(1024)S(1)} %get-tuple-element.64), kind=kCustom, calls=%fused_computation.1.clone | custom fusion | bytes 4194320 | tf_op jit(solution)/shard_map/jit(_take)/gather | solution.py:157
  39.8 0.7 fusion.79
  40.5 0.5 iota_compare_fusion.1
  41.0 0.1 pad_maximum_fusion.4
  41.1 3.4 %collective-permute-start.2 = (bf16[4,544,16]{1,2,0:T(8,128)(2,1)S(1)}, bf16[4,544,16]{1,2,0:T(8,128)(2,1)S(1)}, u32[]{:S(2)}, u32[]{:S(2)}) collective-permute-start(bf16[4,544,16]{1,2,0:T(8,128)(2,1)S(1)} %get-tuple-element.49), channel_id=1, source_target_pairs={{0,1},{1,2},{2,3},{4,5},{5,6},{6,7},{8,9},{9,10},{10,11},{12,13},{... | collective-permute-start | bytes 208904 | tf_op jit(solution)/shard_map/ppermute | solution.py:26
  44.6 1.3 collective-permute-start.3
  45.9 0.5 iota_compare_fusion.2
  46.4 1.7 collective-permute-start.5
  48.1 0.6 copy-done.11
  48.7 2.8 %collective-permute-done.3 = bf16[4,544,16]{1,2,0:T(8,128)(2,1)} collective-permute-done((bf16[4,544,16]{1,2,0:T(8,128)(2,1)S(1)}, bf16[4,544,16]{1,2,0:T(8,128)(2,1)}, u32[]{:S(2)}, u32[]{:S(2)}) %collective-permute-start.3) | collective-permute-done | bytes 69664 | tf_op jit(solution)/shard_map/ppermute | solution.py:27
  51.5 7.6 %fusion.2 = f32[4,512,512]{2,1,0:T(8,128)} fusion(f32[]{:T(128)} %exponential_reduce_fusion.1, bf16[4,544,16]{1,2,0:T(8,128)(2,1)} %collective-permute-done.3, bf16[4,16,512]{1,2,0:T(8,128)(2,1)S(1)} %collective-permute-done.1, bf16[4,512,512]{1,2,0:T(8,128)(2,1)S(1)} %copy-done.1, bf16[4,16,512]{1,2,0:T(8,128)(2,1)S(1)} %collective-permute-done, ...), kind=kOutput, calls=%fused_computation.11 | convolution fusion | flops 2372083712 | bytes 6561796 | tf_op jit(solution)/shard_map/eil,ml->eim/dot_general | solution.py:84
  59.1 7.5 %fusion = f32[4,512,512]{2,1,0:T(8,128)} fusion(f32[]{:T(128)} %exponential_reduce_fusion, bf16[4,544,16]{1,2,0:T(8,128)(2,1)} %collective-permute-done.3, bf16[4,16,512]{1,2,0:T(8,128)(2,1)S(1)} %collective-permute-done.1, bf16[4,512,512]{1,2,0:T(8,128)(2,1)S(1)} %copy-done.1, bf16[4,16,512]{1,2,0:T(8,128)(2,1)S(1)} %collective-permute-done, ...), kind=kOutput, calls=%fused_computation.9 | convolution fusion | flops 2372083712 | bytes 6561796 | tf_op jit(solution)/shard_map/eil,ml->eim/dot_general | solution.py:84
  66.6 1.7 collective-permute-start.6
  68.3 9.5 %multiply_add_fusion = f32[4,512,512]{2,1,0:T(8,128)} fusion(f32[4,512,512]{2,1,0:T(8,128)} %fusion, f32[4,512,512]{2,1,0:T(8,128)} %fusion.2, f32[4]{0:T(128)S(1)} %get-tuple-element.30, f32[4]{0:T(128)S(1)} %get-tuple-element.31, f32[4]{0:T(128)S(1)} %get-tuple-element.29, f32[]{:T(128)} %exponential_reduce_fusion.2, ...), kind=kOutput, calls=%fused_computation.7 | convolution fusion | flops 2377326592 | bytes 14950452 | tf_op jit(solution)/shard_map/eil,ml->eim/dot_general | solution.py:84
  77.8 6.8 %copy.65 = f32[4,512,512]{2,0,1:T(4,128)} copy(f32[4,512,512]{2,1,0:T(8,128)} %multiply_add_fusion) | data formatting | bytes 8388608 | tf_op jit(solution)/shard_map/add | solution.py:85
  84.6 1.9 %gather_fusion.3 = f32[4,32,512]{2,0,1:T(4,128)S(1)} fusion(f32[4,512,512]{2,0,1:T(4,128)} %copy.65, s32[4]{0:T(128)S(1)} %fusion.97), kind=kCustom, calls=%fused_computation.5 | custom fusion | bytes 524336 | tf_op jit(solution)/shard_map/vmap()/gather | solution.py:63
  86.5 1.6 pad_maximum_fusion.1
  88.1 1.1 gather_fusion
  89.3 0.1 copy.64
  89.4 0.7 gather_fusion.1
  90.1 0.4 multiply_reduce_fusion.5
  90.5 0.1 copy.70
  90.6 0.1 copy.71
  90.7 0.1 copy.72
  90.9 27.4 %all-reduce.2 = (f32[4,3,3]{1,2,0:T(4,128)S(1)}, f32[4,3]{0,1:T(4,128)S(1)}) all-reduce(f32[4,3,3]{1,2,0:T(4,128)S(1)} %pad_maximum_fusion.5, f32[4,3]{0,1:T(4,128)S(1)} %pad_maximum_fusion.6), channel_id=1, replica_groups=mesh['visit'=4,'row'=2,'col'=4] {'row','col'}, use_global_device_ids=true, to_apply=%region_16.18 | all-reduce | flops 48 | bytes 384 | tf_op jit(solution)/shard_map/psum | solution.py:146
  118.3 0.1 copy.73
  118.4 1.1 custom-call.4
  119.6 0.7 select_reduce_fusion
  120.2 0.1 compare_reduce_fusion
  120.3 0.1 copy.74
  120.4 0.1 copy.75
  120.5 0.1 copy.76
  120.6 0.7 select_select_fusion
  121.4 0.1 subtract_divide_fusion.1
  121.5 0.2 slice_reduce_fusion.4
  121.8 6.7 %fusion.22 = bf16[4,512,512]{2,1,0:T(8,128)(2,1)} fusion(bf16[4,512,512]{2,1,0:T(8,128)(2,1)} %gather_fusion.5, pred[4]{0:T(512)(128)(4,1)} %get-tuple-element.59, f32[4,512,512]{2,1,0:T(8,128)} %multiply_add_fusion, bf16[4,512,512]{2,1,0:T(8,128)(2,1)S(1)} %copy-done.2, f32[4,512]{1,0:T(4,128)S(1)} %get-tuple-element.67, ...), kind=kOutput, calls=%fused_computation.29 | convolution fusion | flops 2154823680 | bytes 10502152 | tf_op jit(solution)/shard_map/eik,elk->eil/dot_general | solution.py:161
  128.5 4.0 %fusion.27 = bf16[4,512,512]{2,0,1:T(4,128)(2,1)S(1)} fusion(bf16[4,512,512]{2,1,0:T(8,128)(2,1)} %fusion.22, pred[4,4]{1,0:T(4,128)(4,1)S(1)} %copy-done.10, bf16[4]{0:T(256)(128)(2,1)S(1)} %bitcast.149), kind=kOutput, calls=%fused_computation.30 | convolution fusion | flops 9437200 | bytes 4194328 | tf_op jit(solution)/shard_map/ev,eij->vij/dot_general | solution.py:172
  132.5 1.8 copy.79
  134.2 0.1 select_reduce_fusion.2
  134.3 10.7 %all-reduce.1 = bf16[4]{0:T(256)(128)(2,1)S(1)} all-reduce(bf16[4]{0:T(256)(128)(2,1)S(1)} %select_reduce_fusion.2), channel_id=3, replica_groups=mesh['visit'=4,'row'=2,'col'=4] {'visit'}, use_global_device_ids=true, to_apply=%region_21.23.clone | all-reduce | flops 4 | bytes 16
  145.1 0.6 dynamic-slice
  145.6 1.2 dynamic-slice.1
  147.6 0.7 copy.80
  148.2 29.8 %reduce-scatter.2.cloned.1.call-done = bf16[1,512,512]{2,1,0:T(8,128)(2,1)} async-done(((bf16[4,512,512]{2,1,0:T(8,128)(2,1)}), bf16[1,512,512]{2,1,0:T(8,128)(2,1)}) %reduce-scatter.2.cloned.1.call-update) | async-done | bytes 524304 | tf_op jit(solution)/shard_map/reduce_scatter | solution.py:175
  178.0 2.2 %convert_divide_fusion = f32[1,512,512]{2,1,0:T(8,128)} fusion(bf16[1,512,512]{2,1,0:T(8,128)(2,1)} %reduce-scatter.2.cloned.1.call-done, f32[]{:T(128)S(6)} %convert.2), kind=kLoop, calls=%fused_computation.41 | loop fusion | flops 524288 | bytes 1572868 | tf_op jit(solution)/shard_map/div | solution.py:182
  (60 shorter events, 0.6 us)
Async XLA Ops:
  7.2 170.9 %reduce-scatter.2.cloned.1.call-start = ((), (), s32[]{:S(2)}) async-start(), calls=%async_computation.1 | async-start | bytes 2621440 | tf_op jit(solution)/shard_map/reduce_scatter | solution.py:175
  9.1 31.9 %collective-permute-start = (bf16[4,16,512]{1,2,0:T(8,128)(2,1)}, bf16[4,16,512]{1,2,0:T(8,128)(2,1)S(1)}, u32[]{:S(2)}, u32[]{:S(2)}) collective-permute-start(bf16[4,16,512]{1,2,0:T(8,128)(2,1)} %copy.60), channel_id=1, source_target_pairs={{0,4},{1,5},{2,6},{3,7},{8,12},{9,13},{10,14},{11,15},{16,20},{17,... | collective-permute-start | bytes 196616 | tf_op jit(solution)/shard_map/ppermute | solution.py:26
  12.5 28.5 %collective-permute-start.1 = (bf16[4,16,512]{1,2,0:T(8,128)(2,1)}, bf16[4,16,512]{1,2,0:T(8,128)(2,1)S(1)}, u32[]{:S(2)}, u32[]{:S(2)}) collective-permute-start(bf16[4,16,512]{1,2,0:T(8,128)(2,1)} %copy.61), channel_id=1, source_target_pairs={{4,0},{5,1},{6,2},{7,3},{12,8},{13,9},{14,10},{15,11},{20,16},{21,... | collective-permute-start | bytes 196616 | tf_op jit(solution)/shard_map/ppermute | solution.py:27
  13.8 4.7 %copy-start.7 = (s32[8,3]{0,1:T(4,128)S(1)}, s32[8,3]{0,1:T(4,128)}, u32[]{:S(2)}) copy-start(s32[8,3]{0,1:T(4,128)} %param.12) | copy-start | bytes 292
  13.8 9.3 %copy-start = (bf16[4,512,512]{2,1,0:T(8,128)(2,1)S(1)}, bf16[4,512,512]{2,1,0:T(8,128)(2,1)}, u32[]{:S(2)}) copy-start(bf16[4,512,512]{2,1,0:T(8,128)(2,1)} %param.10) | copy-start | bytes 6291460
  20.6 7.4 %copy-start.5 = (f32[4,3]{1,0:T(4,128)S(1)}, f32[4,3]{1,0:T(4,128)}, u32[]{:S(2)}) copy-start(f32[4,3]{1,0:T(4,128)} %param.11) | copy-start | bytes 148
  20.6 8.8 %copy-start.8 = (s32[4,1,1,2]{0,3,2,1:T(2,128)S(1)}, s32[4,1,1,2]{0,3,2,1:T(2,128)}, u32[]{:S(2)}) copy-start(s32[4,1,1,2]{0,3,2,1:T(2,128)} %param.15) | copy-start | bytes 100
  20.6 25.7 %collective-permute-start.4 = (bf16[4,32,512]{2,0,1:T(4,128)(2,1)S(1)}, bf16[4,32,512]{2,0,1:T(4,128)(2,1)S(1)}, u32[]{:S(2)}, u32[]{:S(2)}) collective-permute-start(bf16[4,32,512]{2,0,1:T(4,128)(2,1)S(1)} %gather_fusion.2), channel_id=1, source_target_pairs={{0,8},{8,16},{16,24},{24,0},{1,9},{9,17},{17,25},{25,1},{2,10},{10... | collective-permute-start | bytes 393224 | tf_op jit(solution)/shard_map/ppermute | solution.py:108
  34.7 5.0 %copy-start.13 = (s32[4,1,1]{0,2,1:T(1,128)S(1)}, s32[4,1,1]{0,2,1:T(1,128)}, u32[]{:S(2)}) copy-start(s32[4,1,1]{0,2,1:T(1,128)} %param.17) | copy-start | bytes 52
  34.7 5.1 %copy-start.6 = (s32[4,1,1,4]{3,2,1,0:T(1,128)S(1)}, s32[4,1,1,4]{3,2,1,0:T(1,128)}, u32[]{:S(2)}) copy-start(s32[4,1,1,4]{3,2,1,0:T(1,128)} %param.16) | copy-start | bytes 196
  34.7 6.3 %copy-start.1 = (bf16[4,512,512]{1,2,0:T(8,128)(2,1)S(1)}, bf16[4,512,512]{1,2,0:T(8,128)(2,1)}, u32[]{:S(2)}) copy-start(bf16[4,512,512]{1,2,0:T(8,128)(2,1)} %copy.62) | copy-start | bytes 6291460
  41.1 6.9 %collective-permute-start.2 = (bf16[4,544,16]{1,2,0:T(8,128)(2,1)S(1)}, bf16[4,544,16]{1,2,0:T(8,128)(2,1)S(1)}, u32[]{:S(2)}, u32[]{:S(2)}) collective-permute-start(bf16[4,544,16]{1,2,0:T(8,128)(2,1)S(1)} %get-tuple-element.49), channel_id=1, source_target_pairs={{0,1},{1,2},{2,3},{4,5},{5,6},{6,7},{8,9},{9,10},{10,11},{12,13},{... | collective-permute-start | bytes 208904 | tf_op jit(solution)/shard_map/ppermute | solution.py:26
  44.6 6.9 %collective-permute-start.3 = (bf16[4,544,16]{1,2,0:T(8,128)(2,1)S(1)}, bf16[4,544,16]{1,2,0:T(8,128)(2,1)}, u32[]{:S(2)}, u32[]{:S(2)}) collective-permute-start(bf16[4,544,16]{1,2,0:T(8,128)(2,1)S(1)} %get-tuple-element.50), channel_id=1, source_target_pairs={{1,0},{2,1},{3,2},{5,4},{6,5},{7,6},{9,8},{10,9},{11,10},{13,12},{... | collective-permute-start | bytes 208904 | tf_op jit(solution)/shard_map/ppermute | solution.py:27
  46.4 12.7 %copy-start.3 = (bf16[4,32,512]{2,0,1:T(4,128)(2,1)}, bf16[4,32,512]{2,0,1:T(4,128)(2,1)S(1)}, u32[]{:S(2)}) copy-start(bf16[4,32,512]{2,0,1:T(4,128)(2,1)S(1)} %collective-permute-done.4) | copy-start | bytes 393220
  46.4 20.2 %collective-permute-start.5 = (bf16[4,32,512]{2,0,1:T(4,128)(2,1)S(1)}, bf16[4,32,512]{2,0,1:T(4,128)(2,1)}, u32[]{:S(2)}, u32[]{:S(2)}) collective-permute-start(bf16[4,32,512]{2,0,1:T(4,128)(2,1)S(1)} %collective-permute-done.4), channel_id=1, source_target_pairs={{0,8},{8,16},{16,24},{24,0},{1,9},{9,17},{17,25},{25,1},{2,10},{10... | collective-permute-start | bytes 393224 | tf_op jit(solution)/shard_map/ppermute | solution.py:108
  48.1 0.6 copy-start.11
  51.5 7.6 %copy-start.12 = (bf16[4,544,16]{1,2,0:T(8,128)(2,1)S(1)}, bf16[4,544,16]{1,2,0:T(8,128)(2,1)}, u32[]{:S(2)}) copy-start(bf16[4,544,16]{1,2,0:T(8,128)(2,1)} %copy-done.11) | copy-start | bytes 208900
  66.6 19.9 %collective-permute-start.6 = (bf16[4,32,512]{2,0,1:T(4,128)(2,1)}, bf16[4,32,512]{2,0,1:T(4,128)(2,1)}, u32[]{:S(2)}, u32[]{:S(2)}) collective-permute-start(bf16[4,32,512]{2,0,1:T(4,128)(2,1)} %collective-permute-done.5), channel_id=1, source_target_pairs={{0,8},{8,16},{16,24},{24,0},{1,9},{9,17},{17,25},{25,1},{2,10},{10... | collective-permute-start | bytes 393224 | tf_op jit(solution)/shard_map/ppermute | solution.py:108
  84.6 1.9 %copy-start.4 = (bf16[4,32,512]{2,0,1:T(4,128)(2,1)S(1)}, bf16[4,32,512]{2,0,1:T(4,128)(2,1)}, u32[]{:S(2)}) copy-start(bf16[4,32,512]{2,0,1:T(4,128)(2,1)} %copy-done.3) | copy-start | bytes 393220
  86.5 3.5 %copy-start.9 = (pred[4]{0:T(512)(128)(4,1)S(1)}, pred[4]{0:T(512)(128)(4,1)}, u32[]{:S(2)}) copy-start(pred[4]{0:T(512)(128)(4,1)} %compare_and_fusion.2) | copy-start | bytes 16
  86.5 35.2 %copy-start.2 = (bf16[4,512,512]{2,1,0:T(8,128)(2,1)S(1)}, bf16[4,512,512]{2,1,0:T(8,128)(2,1)}, u32[]{:S(2)}) copy-start(bf16[4,512,512]{2,1,0:T(8,128)(2,1)} %gather_fusion.4) | copy-start | bytes 6291460
  121.7 6.7 %copy-start.10 = (pred[4,4]{1,0:T(4,128)(4,1)S(1)}, pred[4,4]{1,0:T(4,128)(4,1)}, u32[]{:S(2)}) copy-start(pred[4,4]{1,0:T(4,128)(4,1)} %fusion.79) | copy-start | bytes 52
  121.8 6.7 %copy-start.14 = (bf16[4,1,1]{0,2,1:T(2,128)(2,1)S(1)}, bf16[4,1,1]{0,2,1:T(2,128)(2,1)}, u32[]{:S(2)}) copy-start(bf16[4,1,1]{0,2,1:T(2,128)(2,1)} %param.13) | copy-start | bytes 28
  134.2 10.8 %copy-start.15 = (u32[32]{0:T(128)S(1)}, u32[32]{0:T(128)}, u32[]{:S(2)}) copy-start(u32[32]{0:T(128)} %constant.197) | copy-start | bytes 388
Sparse Core Ops, SparseCore 0:
  134.4 43.6 reduce-scatter.1
